TPU v7x, 32 devices: a whole 2x2x4 slice. The times are simulated.
32 devices in a mesh: row: 8 (over z, y), col: 4 (over x, core).
Axes of the slice: x: 2, y: 2, z: 4, core: 2. Of those that a mesh axis runs over, the one named last changes fastest.
Arguments:
- x_scan: float32 [16384, 256], P(('row', 'col')), may hold values from -6 to 6
- owner_slot: int32 [16384], P(('row', 'col')), may hold values from 0 to 16383, as said below
- weight: float32 [256, 256], replicated, may hold values from -0.375 to 0.375
- norm_gain: float32 [256], replicated, may hold values from 0.1 to 1.9
- tile_values: float32 [32, 8, 128, 128], P(('row', 'col')), may hold values from -0.375 to 0.375
- tile_coords: int32 [32, 8, 2], P(('row', 'col')), may hold values from 0 to 3
- counts: int32 [32, 3], P(('row', 'col')), may hold values from 2 to 128, as said below
- boundary_rows: int32 [32, 2, 128], P(('row', 'col')), may hold values from 0 to 511
- coupling: float32 [32, 2, 128, 128], P(('row', 'col')), may hold values from -0.5 to 0.5
- cotangent: float32 [16384, 256], P(('row', 'col')), may hold values from -6 to 6
Outputs:
- output: float32 [16384, 256], P(('row', 'col'))
- x_grad: float32 [16384, 256], P(('row', 'col'))
- weight_grad: float32 [256, 256], replicated
- gain_grad: float32 [256], replicated
Inputs may be any that keep to these rules, and one draw needn't show every extreme that they name: Each value appears once. The scan rows of one partition go to partition owner_slot // 512: exactly 32 of them to one partition, none to another, and 16 to each of the rest. `counts`: column 0 lies between 2 and 8 and equals 8 on some partition; every other column lies between 32 and 128 and equals 128 on some partition.
All inputs are finite; a program needn't handle non-finite values.
Results may differ from a plain program's by a relative error of at most 0.0003.
Values sent between devices are 32-bit elements; how exact they have to be, the bound alone decides.
No kernel may reach another device: no remote copies, remote signals or barrier semaphores. Data moves between devices by JAX's collectives and lax.ppermute only.
A program may use at most 64 MiB of HBM per device.

v0:
```python
import math
import jax
import jax.numpy as jnp
from jax import lax
from jax.sharding import PartitionSpec as P

BLOCK = 128
ROUNDS = 2
EPS = 1e-05
PRECISE = lax.Precision.HIGHEST


def swapped(array, axis, apart):
    return lax.ppermute(array, axis, [(i, i ^ 1 << apart) for i in range(lax.axis_size(axis))])


def layer_piece(aggregate, weight, norm_gain):
    inv_scale = lax.rsqrt(jnp.mean(aggregate * aggregate, axis=-1, keepdims=True) + EPS)
    normed = aggregate * inv_scale * norm_gain
    return jax.nn.silu(
        jnp.dot(normed, weight, precision=PRECISE, preferred_element_type=jnp.float32)
    )


def interior(hidden, tile_values, tile_coords, live_count, transpose):
    feat_count = hidden.shape[1]
    blocks = hidden.reshape(-1, BLOCK, feat_count)
    if transpose:
        source_col, target_col, form = (0, 1, "tji,tjf->tif")
    else:
        source_col, target_col, form = (1, 0, "tij,tjf->tif")
    live_mask = (jnp.arange(tile_values.shape[0]) < live_count).astype(jnp.float32)
    source = blocks[tile_coords[:, source_col]]
    product = jnp.einsum(form, tile_values * live_mask[:, None, None], source, precision=PRECISE)
    result = jnp.zeros_like(blocks).at[tile_coords[:, target_col]].add(product)
    return result.reshape(hidden.shape)


def boundary_forward(total, hidden, boundary_rows, coupling, counts):
    for round_index in range(ROUNDS):
        picked = boundary_rows[0, round_index]
        own_mask = (jnp.arange(BLOCK) < counts[0, 1 + round_index]).astype(jnp.float32)[:, None]
        outgoing = hidden[picked] * own_mask
        received = swapped(outgoing, "col", round_index)
        contrib = (
            jnp.dot(
                coupling[0, round_index],
                received,
                precision=PRECISE,
                preferred_element_type=jnp.float32,
            )
            * own_mask
        )
        total = total.at[picked].add(contrib)
    return total


def boundary_backward(total, grad_agg, boundary_rows, coupling, counts):
    for round_index in range(ROUNDS):
        picked = boundary_rows[0, round_index]
        own_mask = (jnp.arange(BLOCK) < counts[0, 1 + round_index]).astype(jnp.float32)[:, None]
        outgoing = grad_agg[picked] * own_mask
        carried = jnp.dot(
            coupling[0, round_index].T,
            outgoing,
            precision=PRECISE,
            preferred_element_type=jnp.float32,
        )
        received = swapped(carried, "col", round_index)
        total = total.at[picked].add(received * own_mask)
    return total


def on_device(
    x_scan,
    owner_slot,
    weight,
    norm_gain,
    tile_values,
    tile_coords,
    counts,
    boundary_rows,
    coupling,
    cotangent,
):
    row_count, feat_count = x_scan.shape
    grid_rows = lax.axis_size("row")
    grid_cols = lax.axis_size("col")
    devices = grid_rows * grid_cols
    capacity = 2 * row_count // devices
    target = owner_slot // row_count
    within = owner_slot % row_count
    sorting = jnp.argsort(target, stable=True)
    sorted_target = target[sorting]
    per_peer = jnp.sum(
        (target[:, None] == jnp.arange(devices, dtype=jnp.int32)[None, :]).astype(jnp.int32), axis=0
    )
    starts = jnp.cumsum(per_peer) - per_peer
    ranked = (
        jnp.zeros((row_count,), jnp.int32)
        .at[sorting]
        .set(jnp.arange(row_count, dtype=jnp.int32) - starts[sorted_target])
    )
    bucket = target * capacity + ranked
    outbox = jnp.zeros((devices * capacity, feat_count), jnp.float32).at[bucket].set(x_scan)
    places = jnp.full((devices * capacity,), row_count, jnp.int32).at[bucket].set(within)
    inbox, place_in = (
        lax.all_to_all(
            outbox.reshape(devices, capacity, feat_count),
            ("row", "col"),
            split_axis=0,
            concat_axis=0,
            tiled=True,
        ),
        lax.all_to_all(
            places.reshape(devices, capacity),
            ("row", "col"),
            split_axis=0,
            concat_axis=0,
            tiled=True,
        ),
    )
    inbox = inbox.reshape(-1, feat_count)
    place_in = place_in.reshape(-1)
    hidden = jnp.zeros((row_count, feat_count), jnp.float32).at[place_in].set(inbox, mode="drop")
    aggregate = hidden + interior(hidden, tile_values[0], tile_coords[0], counts[0, 0], False)
    aggregate = boundary_forward(aggregate, hidden, boundary_rows, coupling, counts)
    activation, pullback = jax.vjp(layer_piece, aggregate, weight, norm_gain)
    output = hidden + activation
    grad_agg, grad_weight, grad_gain = pullback(cotangent)
    weight_sum, gain_sum = lax.psum((grad_weight, grad_gain), ("row", "col"))
    grad_nodes = (
        cotangent
        + grad_agg
        + interior(grad_agg, tile_values[0], tile_coords[0], counts[0, 0], True)
    )
    grad_nodes = boundary_backward(grad_nodes, grad_agg, boundary_rows, coupling, counts)
    valid = (place_in < row_count).astype(jnp.float32)[:, None]
    reply = grad_nodes[jnp.minimum(place_in, row_count - 1)] * valid
    returned = lax.all_to_all(
        reply.reshape(devices, capacity, feat_count),
        ("row", "col"),
        split_axis=0,
        concat_axis=0,
        tiled=True,
    )
    x_grad = returned.reshape(-1, feat_count)[bucket]
    node_scale = 1.0 / math.sqrt(row_count * devices)
    return (output, x_grad, weight_sum * node_scale, gain_sum * node_scale)


def solution(mesh):
    in_specs = (
        P(("row", "col"), None),
        P(("row", "col")),
        P(),
        P(),
        P(("row", "col"), None, None, None),
        P(("row", "col"), None, None),
        P(("row", "col"), None),
        P(("row", "col"), None, None),
        P(("row", "col"), None, None, None),
        P(("row", "col"), None),
    )
    out_specs = (P(("row", "col"), None), P(("row", "col"), None), P(), P())
    return jax.shard_map(
        on_device, mesh=mesh, in_specs=in_specs, out_specs=out_specs, check_vma=False
    )
```

profile of v0, /device:TPU:0, one launch (start us, length us, event | category | flops | bytes accessed | tf_op | source)
XLA Modules:
  0.0 280.3 jit_solution(10291379477697038767)
XLA Ops:
  9.8 3.8 %sort.17 = (s32[512]{0:T(512)}, s32[512]{0:T(512)S(1)}) sort(s32[512]{0:T(512)S(1)} %get-tuple-element.38, s32[512]{0:T(512)S(1)} %iota.29), dimensions={0}, to_apply=%region_0.1 | sort | flops 4608 | bytes 8192 | tf_op jit(solution)/shard_map/jit(argsort)/sort | solution.py:93
  13.5 3.5 %gather_fusion = s32[512]{0:T(512)S(1)} fusion(s32[512]{0:T(512)S(1)} %get-tuple-element.38, s32[1024]{0:T(1024)S(1)} %pad_clamp_fusion.5), kind=kCustom, calls=%fused_computation | custom fusion | bytes 6144 | tf_op jit(solution)/shard_map/gather | solution.py:94
  17.0 4.3 %compare_select_fusion.3 = (s32[512,1]{0,1:T(1,128)S(1)}, s32[512,1]{0,1:T(1,128)S(1)}) fusion(s32[]{:T(128)} %bitcast.27, s32[]{:T(128)} %bitcast.28, s32[]{:T(128)} %bitcast.29, s32[]{:T(128)} %bitcast.30, s32[]{:T(128)} %bitcast.31, s32[]{:T(128)} %bitcast.33, s32[]{:T(128)} %bitcast.32, s32[512,1]{0,1:T(1,128)S(1)} %bitcast.100), kind=kLoop, calls=%fused_computation.104 | loop fusion | flops 7680 | bytes 6172 | tf_op jit(solution)/shard_map/gather | solution.py:102
  21.5 15.8 %select_subtract_fusion = s32[512]{0:T(512)S(1)} fusion(pred[512]{0:T(512)(128)(4,1)S(1)} %get-tuple-element.32, pred[512]{0:T(512)(128)(4,1)S(1)} %get-tuple-element.31, pred[512]{0:T(512)(128)(4,1)S(1)} %get-tuple-element.30, pred[512]{0:T(512)(128)(4,1)S(1)} %get-tuple-element.29, pred[512]{0:T(512)(128)(4,1)S(1)} %get-tuple-element.28, ...), kind=kLoop, calls=%fused_computation.128 | loop fusion | flops 13312 | bytes 16996 | tf_op jit(solution)/shard_map/sub | solution.py:102
  37.3 2.4 scatter_custom_fusion
  39.7 2.4 scatter_custom_fusion.1
  42.9 7.3 %all-to-all-start = ((s32[32,1,32]{2,1,0:T(1,128)}), s32[32,1,32]{2,1,0:T(1,128)S(1)}, u32[]{:S(2)}, u32[]{:S(2)}) async-start(s32[32,1,32]{2,1,0:T(1,128)} %all_to_all.12), calls=%async_computation | async-start | bytes 32768 | tf_op jit(solution)/shard_map/all_to_all | solution.py:115
  50.2 3.7 %scatter_custom_fusion.2 = f32[1024,256]{1,0:T(8,128)} fusion(s32[512]{0:T(512)S(1)} %compare_select_fusion.9, f32[512,256]{1,0:T(8,128)} %param.10, f32[]{:T(128)} %constant.21.clone.1), kind=kCustom, calls=%fused_computation.38 | custom fusion | bytes 1049088 | tf_op jit(solution)/shard_map/scatter | solution.py:105
  53.9 3.3 %all-to-all-done = s32[32,1,32]{2,1,0:T(1,128)S(1)} async-done(((s32[32,1,32]{2,1,0:T(1,128)}), s32[32,1,32]{2,1,0:T(1,128)S(1)}, u32[]{:S(2)}, u32[]{:S(2)}) %all-to-all-start) | async-done | bytes 4128 | tf_op jit(solution)/shard_map/all_to_all | solution.py:115
  57.3 2.8 all-to-all-start.1
  65.3 20.9 %all-to-all-done.1 = f32[32,32,256]{2,1,0:T(8,128)S(1)} async-done(((f32[32,32,256]{2,1,0:T(8,128)}), f32[32,32,256]{2,1,0:T(8,128)S(1)}, u32[]{:S(2)}, u32[]{:S(2)}) %all-to-all-start.1) | async-done | bytes 1048608 | tf_op jit(solution)/shard_map/all_to_all | solution.py:108
  86.3 4.9 %scatter_custom_fusion.3 = f32[512,256]{1,0:T(8,128)S(1)} fusion(s32[1024]{0:T(1024)S(1)} %bitcast.101, f32[1024,256]{1,0:T(8,128)S(1)} %bitcast.96, f32[]{:T(128)} %constant.21.clone.1), kind=kCustom, calls=%fused_computation.54 | custom fusion | bytes 524292 | tf_op jit(solution)/shard_map/scatter | solution.py:125
  98.5 4.0 %collective-permute-done.1 = f32[128,256]{0,1:T(8,128)S(1)} collective-permute-done((f32[128,256]{0,1:T(8,128)S(1)}, f32[128,256]{0,1:T(8,128)S(1)}, u32[]{:S(2)}, u32[]{:S(2)}) %collective-permute-start.1) | collective-permute-done | bytes 131104 | tf_op jit(solution)/shard_map/ppermute | solution.py:14
  102.9 1.7 scatter_fusion.1
  112.1 2.1 fusion.6
  114.2 2.5 scatter_fusion.3
  119.3 4.3 %collective-permute-done.3 = f32[128,256]{0,1:T(8,128)S(1)} collective-permute-done((f32[128,256]{0,1:T(8,128)S(1)}, f32[128,256]{0,1:T(8,128)S(1)}, u32[]{:S(2)}, u32[]{:S(2)}) %collective-permute-start.3) | collective-permute-done | bytes 131104 | tf_op jit(solution)/shard_map/ppermute | solution.py:14
  126.7 3.5 %gather_fusion.7 = f32[1024,256]{1,0:T(8,128)S(1)} fusion(f32[512,256]{1,0:T(8,128)S(1)} %scatter_fusion.5, s32[1024]{0:T(1024)S(1)} %broadcast_clamp_fusion), kind=kCustom, calls=%fused_computation.7 | custom fusion | bytes 2101248 | tf_op jit(solution)/shard_map/gather | solution.py:139
  131.4 3.5 %all-to-all-start.2 = ((f32[32,32,256]{2,1,0:T(8,128)}), f32[32,32,256]{2,1,0:T(8,128)S(1)}, u32[]{:S(2)}, u32[]{:S(2)}) async-start(f32[32,32,256]{2,1,0:T(8,128)} %broadcast_multiply_fusion), calls=%async_computation.2 | async-start | bytes 2097152 | tf_op jit(solution)/shard_map/all_to_all | solution.py:140
  135.0 1.9 fusion.8
  136.9 45.2 %psum.15 = f32[256]{0:T(256)S(1)} all-reduce(f32[256]{0:T(256)S(1)} %get-tuple-element.6), channel_id=1, replica_groups=mesh['row'=8,'col'=4] {'row','col'}, use_global_device_ids=true, to_apply=%region_17.18 | all-reduce | flops 256 | bytes 2048 | tf_op jit(solution)/shard_map/psum | solution.py:131
  182.6 86.9 %all-reduce.2.cloned.1.call-done = f32[256,256]{1,0:T(8,128)} async-done(((f32[256,256]{1,0:T(8,128)}), f32[256,256]{1,0:T(8,128)}) %all-reduce.2.cloned.1.call-update) | async-done | bytes 262160 | tf_op jit(solution)/shard_map/psum | solution.py:131
  269.5 1.7 broadcast_multiply_fusion.1
  271.2 2.2 gather_fusion.8
  (101 shorter events, 31.1 us)
Async XLA Ops:
  7.2 99.1 %copy-start = (f32[256,256]{1,0:T(8,128)S(1)}, f32[256,256]{1,0:T(8,128)}, u32[]{:S(2)}) copy-start(f32[256,256]{1,0:T(8,128)} %param.12) | copy-start | bytes 786436
  42.9 14.4 %all-to-all-start = ((s32[32,1,32]{2,1,0:T(1,128)}), s32[32,1,32]{2,1,0:T(1,128)S(1)}, u32[]{:S(2)}, u32[]{:S(2)}) async-start(s32[32,1,32]{2,1,0:T(1,128)} %all_to_all.12), calls=%async_computation | async-start | bytes 32768 | tf_op jit(solution)/shard_map/all_to_all | solution.py:115
  57.2 2.8 copy-start.6
  57.3 29.0 %all-to-all-start.1 = ((f32[32,32,256]{2,1,0:T(8,128)}), f32[32,32,256]{2,1,0:T(8,128)S(1)}, u32[]{:S(2)}, u32[]{:S(2)}) async-start(f32[32,32,256]{2,1,0:T(8,128)} %bitcast.36), calls=%async_computation.1 | async-start | bytes 2097152 | tf_op jit(solution)/shard_map/all_to_all | solution.py:108
  62.6 0.7 copy-start.7
  63.3 0.7 copy-start.8
  91.2 1.0 copy-start.1
  95.6 2.5 collective-permute-start
  96.6 1.6 copy-start.3
  96.6 6.0 %collective-permute-start.1 = (f32[128,256]{0,1:T(8,128)S(1)}, f32[128,256]{0,1:T(8,128)S(1)}, u32[]{:S(2)}, u32[]{:S(2)}) collective-permute-start(f32[128,256]{0,1:T(8,128)S(1)} %broadcast_multiply_fusion.3), channel_id=1, source_target_pairs={{0,2},{1,3},{2,0},{3,1},{4,6},{5,7},{6,4},{7,5},{8,10},{9,11},{10,... | collective-permute-start | bytes 393224 | tf_op jit(solution)/shard_map/ppermute | solution.py:14
  106.3 0.7 copy-start.9
  107.0 1.5 copy-start.4
  108.4 0.9 copy-start.10
  111.0 1.0 copy-start.2
  114.2 2.5 copy-start.5
  117.2 2.0 collective-permute-start.2
  117.6 6.0 %collective-permute-start.3 = (f32[128,256]{0,1:T(8,128)S(1)}, f32[128,256]{0,1:T(8,128)S(1)}, u32[]{:S(2)}, u32[]{:S(2)}) collective-permute-start(f32[128,256]{0,1:T(8,128)S(1)} %convolution_bitcast_fusion), channel_id=1, source_target_pairs={{0,2},{1,3},{2,0},{3,1},{4,6},{5,7},{6,4},{7,5},{8,10},{9,11},{10,... | collective-permute-start | bytes 393224 | tf_op jit(solution)/shard_map/ppermute | solution.py:14
  131.4 3.6 %copy-start.11 = (f32[512,256]{1,0:T(8,128)S(1)}, f32[512,256]{1,0:T(8,128)}, u32[]{:S(2)}) copy-start(f32[512,256]{1,0:T(8,128)} %copy-done.10) | copy-start | bytes 1572868
  131.4 139.8 %all-to-all-start.2 = ((f32[32,32,256]{2,1,0:T(8,128)}), f32[32,32,256]{2,1,0:T(8,128)S(1)}, u32[]{:S(2)}, u32[]{:S(2)}) async-start(f32[32,32,256]{2,1,0:T(8,128)} %broadcast_multiply_fusion), calls=%async_computation.2 | async-start | bytes 2097152 | tf_op jit(solution)/shard_map/all_to_all | solution.py:140
  134.9 134.6 %all-reduce.2.cloned.1.call-start = ((), (), s32[]{:S(2)}) async-start(), calls=%async_computation.3 | async-start | bytes 524288 | tf_op jit(solution)/shard_map/psum | solution.py:131
Sparse Core Ops, SparseCore 0:
  141.9 127.6 all-reduce.1
where the time goes:
time: 281 us; the launch traced here: 280 us
  waiting for transfers between devices  119 us (42%)
  blocking collectives  45.2 us (16%)
  other arithmetic  41.7 us (15%)
  local copies, waits for them, and re-layouts  34 us (12%)
  starting transfers between devices  16.9 us (6%)
  between operations  14.6 us (5%)
  matrix products  8.46 us (3%)
    psum x1, waiting for transfers between devices, on_device(): weight_sum, gain_sum = lax.psum((grad_weight, grad_gain), ('row', 'col'))  86.9 us
    psum x1, blocking collectives, on_device(): weight_sum, gain_sum = lax.psum((grad_weight, grad_gain), ('row', 'col'))  45.2 us
    all_to_all x1, waiting for transfers between devices, on_device(): lax.all_to_all(outbox.reshape(devices, capacity, feat_count), ('row', 'co...  20.9 us
    sub x1, other arithmetic, on_device(): jnp.arange(row_count, dtype=jnp.int32) - starts[sorted_target]  15.8 us
    ppermute x4, waiting for transfers between devices, swapped(): lax.ppermute(array, axis, [(i, i ^ 1 << apart) for i in range(lax.axis_si...  8.32 us
    all_to_all x1, starting transfers between devices, on_device(): lax.all_to_all(places.reshape(devices, capacity), ('row', 'col'), split_a...  7.3 us
  transfers between devices with their start and end apart: 8, of which 5 were waited for; matrix products, arithmetic and copies ran while one was open for 5% of the time, Pallas kernels for 0%

commit v1 on v0

--- a/solution.py
+++ b/solution.py
@@ -8,6 +8,11 @@
 ROUNDS = 2
 EPS = 1e-05
 PRECISE = lax.Precision.HIGHEST
+
+
+def axis_by_axis(array_2, inner_axis, outer_axis):
+    partial = lax.psum(array_2, inner_axis)
+    return lax.psum(partial, outer_axis)
 
 
 def swapped(array, axis, apart):
@@ -128,7 +133,7 @@
     activation, pullback = jax.vjp(layer_piece, aggregate, weight, norm_gain)
     output = hidden + activation
     grad_agg, grad_weight, grad_gain = pullback(cotangent)
-    weight_sum, gain_sum = lax.psum((grad_weight, grad_gain), ("row", "col"))
+    weight_sum, gain_sum = axis_by_axis((grad_weight, grad_gain), "col", "row")
     grad_nodes = (
         cotangent
         + grad_agg

time: 281 us -> 258 us (0.918)
  blocking collectives: 45.2 us -> 27.1 us
  waiting for transfers between devices: 119 us -> 114 us
    psum x1 -> x2, blocking collectives: 45.2 us -> 27.1 us  [the longest x1 21.4 us: axis_by_axis(): return lax.psum(partial, outer_axis)]
    psum x1 -> x2, waiting for transfers between devices: 86.9 us -> 81.8 us  [the longest x1 46.6 us: axis_by_axis(): return lax.psum(partial, outer_axis)]
  transfers between devices with their start and end apart: 8 -> 9, of which waited for: 5 -> 6; matrix products, arithmetic and copies ran while one was open for 5% -> 5% of each run, Pallas kernels for 0% -> 0%
where the time goes in v1:
time: 258 us; the launch traced here: 257 us
  waiting for transfers between devices  114 us (44%)
  other arithmetic  41.7 us (16%)
  local copies, waits for them, and re-layouts  34 us (13%)
  blocking collectives  27.1 us (11%)
  starting transfers between devices  16.9 us (7%)
  between operations  14.6 us (6%)
  matrix products  8.45 us (3%)
    psum x1, waiting for transfers between devices, axis_by_axis(): return lax.psum(partial, outer_axis)  46.6 us
    psum x1, waiting for transfers between devices, axis_by_axis(): partial = lax.psum(array_2, inner_axis)  35.2 us
    psum x1, blocking collectives, axis_by_axis(): return lax.psum(partial, outer_axis)  21.4 us
    all_to_all x1, waiting for transfers between devices, on_device(): lax.all_to_all(outbox.reshape(devices, capacity, feat_count), ('row', 'co...  20.9 us
    sub x1, other arithmetic, on_device(): jnp.arange(row_count, dtype=jnp.int32) - starts[sorted_target]  15.8 us
    ppermute x4, waiting for transfers between devices, swapped(): lax.ppermute(array, axis, [(i, i ^ 1 << apart) for i in range(lax.axis_si...  8.31 us
    all_to_all x1, starting transfers between devices, on_device(): lax.all_to_all(places.reshape(devices, capacity), ('row', 'col'), split_a...  7.3 us
    psum x1, blocking collectives, axis_by_axis(): partial = lax.psum(array_2, inner_axis)  5.76 us
  transfers between devices with their start and end apart: 9, of which 6 were waited for; matrix products, arithmetic and copies ran while one was open for 5% of the time, Pallas kernels for 0%

profile of v1, /device:TPU:0, one launch (start us, length us, event | category | flops | bytes accessed | tf_op | source)
XLA Modules:
  0.0 257.2 jit_solution(15490960518410638754)
XLA Ops:
  9.8 3.8 %sort.17 = (s32[512]{0:T(512)}, s32[512]{0:T(512)S(1)}) sort(s32[512]{0:T(512)S(1)} %get-tuple-element.38, s32[512]{0:T(512)S(1)} %iota.29), dimensions={0}, to_apply=%region_0.1 | sort | flops 4608 | bytes 8192 | tf_op jit(solution)/shard_map/jit(argsort)/sort | solution.py:98
  13.5 3.5 %gather_fusion = s32[512]{0:T(512)S(1)} fusion(s32[512]{0:T(512)S(1)} %get-tuple-element.38, s32[1024]{0:T(1024)S(1)} %pad_clamp_fusion.5), kind=kCustom, calls=%fused_computation | custom fusion | bytes 6144 | tf_op jit(solution)/shard_map/gather | solution.py:99
  17.0 4.3 %compare_select_fusion.3 = (s32[512,1]{0,1:T(1,128)S(1)}, s32[512,1]{0,1:T(1,128)S(1)}) fusion(s32[]{:T(128)} %bitcast.27, s32[]{:T(128)} %bitcast.28, s32[]{:T(128)} %bitcast.29, s32[]{:T(128)} %bitcast.30, s32[]{:T(128)} %bitcast.31, s32[]{:T(128)} %bitcast.33, s32[]{:T(128)} %bitcast.32, s32[512,1]{0,1:T(1,128)S(1)} %bitcast.100), kind=kLoop, calls=%fused_computation.104 | loop fusion | flops 7680 | bytes 6172 | tf_op jit(solution)/shard_map/gather | solution.py:107
  21.5 15.8 %select_subtract_fusion = s32[512]{0:T(512)S(1)} fusion(pred[512]{0:T(512)(128)(4,1)S(1)} %get-tuple-element.32, pred[512]{0:T(512)(128)(4,1)S(1)} %get-tuple-element.31, pred[512]{0:T(512)(128)(4,1)S(1)} %get-tuple-element.30, pred[512]{0:T(512)(128)(4,1)S(1)} %get-tuple-element.29, pred[512]{0:T(512)(128)(4,1)S(1)} %get-tuple-element.28, ...), kind=kLoop, calls=%fused_computation.128 | loop fusion | flops 13312 | bytes 16996 | tf_op jit(solution)/shard_map/sub | solution.py:107
  37.3 2.4 scatter_custom_fusion
  39.7 2.4 scatter_custom_fusion.1
  42.9 7.3 %all-to-all-start = ((s32[32,1,32]{2,1,0:T(1,128)}), s32[32,1,32]{2,1,0:T(1,128)S(1)}, u32[]{:S(2)}, u32[]{:S(2)}) async-start(s32[32,1,32]{2,1,0:T(1,128)} %all_to_all.12), calls=%async_computation | async-start | bytes 32768 | tf_op jit(solution)/shard_map/all_to_all | solution.py:120
  50.2 3.7 %scatter_custom_fusion.2 = f32[1024,256]{1,0:T(8,128)} fusion(s32[512]{0:T(512)S(1)} %compare_select_fusion.9, f32[512,256]{1,0:T(8,128)} %param.10, f32[]{:T(128)} %constant.21.clone.1), kind=kCustom, calls=%fused_computation.38 | custom fusion | bytes 1049088 | tf_op jit(solution)/shard_map/scatter | solution.py:110
  53.9 3.3 %all-to-all-done = s32[32,1,32]{2,1,0:T(1,128)S(1)} async-done(((s32[32,1,32]{2,1,0:T(1,128)}), s32[32,1,32]{2,1,0:T(1,128)S(1)}, u32[]{:S(2)}, u32[]{:S(2)}) %all-to-all-start) | async-done | bytes 4128 | tf_op jit(solution)/shard_map/all_to_all | solution.py:120
  57.3 2.8 %all-to-all-start.1 = ((f32[32,32,256]{2,1,0:T(8,128)}), f32[32,32,256]{2,1,0:T(8,128)S(1)}, u32[]{:S(2)}, u32[]{:S(2)}) async-start(f32[32,32,256]{2,1,0:T(8,128)} %bitcast.36), calls=%async_computation.1 | async-start | bytes 2097152 | tf_op jit(solution)/shard_map/all_to_all | solution.py:113
  65.3 20.9 %all-to-all-done.1 = f32[32,32,256]{2,1,0:T(8,128)S(1)} async-done(((f32[32,32,256]{2,1,0:T(8,128)}), f32[32,32,256]{2,1,0:T(8,128)S(1)}, u32[]{:S(2)}, u32[]{:S(2)}) %all-to-all-start.1) | async-done | bytes 1048608 | tf_op jit(solution)/shard_map/all_to_all | solution.py:113
  86.3 4.9 %scatter_custom_fusion.3 = f32[512,256]{1,0:T(8,128)S(1)} fusion(s32[1024]{0:T(1024)S(1)} %bitcast.101, f32[1024,256]{1,0:T(8,128)S(1)} %bitcast.96, f32[]{:T(128)} %constant.21.clone.1), kind=kCustom, calls=%fused_computation.54 | custom fusion | bytes 524292 | tf_op jit(solution)/shard_map/scatter | solution.py:130
  98.5 4.0 %collective-permute-done.1 = f32[128,256]{0,1:T(8,128)S(1)} collective-permute-done((f32[128,256]{0,1:T(8,128)S(1)}, f32[128,256]{0,1:T(8,128)S(1)}, u32[]{:S(2)}, u32[]{:S(2)}) %collective-permute-start.1) | collective-permute-done | bytes 131104 | tf_op jit(solution)/shard_map/ppermute | solution.py:19
  112.1 2.1 fusion.6
  114.2 2.5 scatter_fusion.3
  119.3 4.3 %collective-permute-done.3 = f32[128,256]{0,1:T(8,128)S(1)} collective-permute-done((f32[128,256]{0,1:T(8,128)S(1)}, f32[128,256]{0,1:T(8,128)S(1)}, u32[]{:S(2)}, u32[]{:S(2)}) %collective-permute-start.3) | collective-permute-done | bytes 131104 | tf_op jit(solution)/shard_map/ppermute | solution.py:19
  126.7 3.5 %gather_fusion.7 = f32[1024,256]{1,0:T(8,128)S(1)} fusion(f32[512,256]{1,0:T(8,128)S(1)} %scatter_fusion.5, s32[1024]{0:T(1024)S(1)} %broadcast_clamp_fusion), kind=kCustom, calls=%fused_computation.7 | custom fusion | bytes 2101248 | tf_op jit(solution)/shard_map/gather | solution.py:144
  131.4 3.5 %all-to-all-start.2 = ((f32[32,32,256]{2,1,0:T(8,128)}), f32[32,32,256]{2,1,0:T(8,128)S(1)}, u32[]{:S(2)}, u32[]{:S(2)}) async-start(f32[32,32,256]{2,1,0:T(8,128)} %broadcast_multiply_fusion), calls=%async_computation.2 | async-start | bytes 2097152 | tf_op jit(solution)/shard_map/all_to_all | solution.py:145
  135.0 1.9 fusion.8
  136.9 35.2 %all-reduce.3.cloned.1.call-done = f32[256,256]{1,0:T(8,128)} async-done(((f32[256,256]{1,0:T(8,128)}), f32[256,256]{1,0:T(8,128)}) %all-reduce.3.cloned.1.call-update) | async-done | bytes 262160 | tf_op jit(solution)/shard_map/psum | solution.py:14
  172.2 5.8 %psum.30 = f32[256]{0:T(256)S(1)} all-reduce(f32[256]{0:T(256)S(1)} %get-tuple-element.6), channel_id=1, replica_groups=mesh['row'=8,'col'=4] {'col'}, use_global_device_ids=true, to_apply=%region_18.19 | all-reduce | flops 256 | bytes 2048 | tf_op jit(solution)/shard_map/psum | solution.py:14
  177.9 21.4 %psum.31 = f32[256]{0:T(256)S(1)} all-reduce(f32[256]{0:T(256)S(1)} %psum.30), channel_id=1, replica_groups=mesh['row'=8,'col'=4] {'row'}, use_global_device_ids=true, to_apply=%region_19.20 | all-reduce | flops 256 | bytes 2048 | tf_op jit(solution)/shard_map/psum | solution.py:15
  199.9 46.6 %all-reduce.5.cloned.1.call-done = f32[256,256]{1,0:T(8,128)} async-done(((f32[256,256]{1,0:T(8,128)}), f32[256,256]{1,0:T(8,128)}) %all-reduce.5.cloned.1.call-update) | async-done | bytes 262160 | tf_op jit(solution)/shard_map/psum | solution.py:15
  248.2 2.2 gather_fusion.8
  (105 shorter events, 34.5 us)
Async XLA Ops:
  7.2 99.1 %copy-start = (f32[256,256]{1,0:T(8,128)S(1)}, f32[256,256]{1,0:T(8,128)}, u32[]{:S(2)}) copy-start(f32[256,256]{1,0:T(8,128)} %param.12) | copy-start | bytes 786436
  42.9 14.4 %all-to-all-start = ((s32[32,1,32]{2,1,0:T(1,128)}), s32[32,1,32]{2,1,0:T(1,128)S(1)}, u32[]{:S(2)}, u32[]{:S(2)}) async-start(s32[32,1,32]{2,1,0:T(1,128)} %all_to_all.12), calls=%async_computation | async-start | bytes 32768 | tf_op jit(solution)/shard_map/all_to_all | solution.py:120
  57.2 2.8 %copy-start.6 = (s32[1,3]{1,0:T(1,128)S(1)}, s32[1,3]{1,0:T(1,128)}, u32[]{:S(2)}) copy-start(s32[1,3]{1,0:T(1,128)} %param.16) | copy-start | bytes 40
  57.3 29.0 %all-to-all-start.1 = ((f32[32,32,256]{2,1,0:T(8,128)}), f32[32,32,256]{2,1,0:T(8,128)S(1)}, u32[]{:S(2)}, u32[]{:S(2)}) async-start(f32[32,32,256]{2,1,0:T(8,128)} %bitcast.36), calls=%async_computation.1 | async-start | bytes 2097152 | tf_op jit(solution)/shard_map/all_to_all | solution.py:113
  62.6 0.7 copy-start.7
  63.3 0.7 copy-start.8
  91.2 1.0 copy-start.1
  95.6 2.5 collective-permute-start
  96.6 1.6 copy-start.3
  96.6 6.0 %collective-permute-start.1 = (f32[128,256]{0,1:T(8,128)S(1)}, f32[128,256]{0,1:T(8,128)S(1)}, u32[]{:S(2)}, u32[]{:S(2)}) collective-permute-start(f32[128,256]{0,1:T(8,128)S(1)} %broadcast_multiply_fusion.3), channel_id=1, source_target_pairs={{0,2},{1,3},{2,0},{3,1},{4,6},{5,7},{6,4},{7,5},{8,10},{9,11},{10,... | collective-permute-start | bytes 393224 | tf_op jit(solution)/shard_map/ppermute | solution.py:19
  106.3 0.7 copy-start.9
  107.0 1.5 copy-start.4
  108.4 0.8 copy-start.10
  111.0 1.0 copy-start.2
  114.2 2.5 copy-start.5
  117.2 2.0 collective-permute-start.2
  117.6 6.0 %collective-permute-start.3 = (f32[128,256]{0,1:T(8,128)S(1)}, f32[128,256]{0,1:T(8,128)S(1)}, u32[]{:S(2)}, u32[]{:S(2)}) collective-permute-start(f32[128,256]{0,1:T(8,128)S(1)} %convolution_bitcast_fusion), channel_id=1, source_target_pairs={{0,2},{1,3},{2,0},{3,1},{4,6},{5,7},{6,4},{7,5},{8,10},{9,11},{10,... | collective-permute-start | bytes 393224 | tf_op jit(solution)/shard_map/ppermute | solution.py:19
  131.4 3.6 %copy-start.11 = (f32[512,256]{1,0:T(8,128)S(1)}, f32[512,256]{1,0:T(8,128)}, u32[]{:S(2)}) copy-start(f32[512,256]{1,0:T(8,128)} %copy-done.10) | copy-start | bytes 1572868
  131.4 116.8 %all-to-all-start.2 = ((f32[32,32,256]{2,1,0:T(8,128)}), f32[32,32,256]{2,1,0:T(8,128)S(1)}, u32[]{:S(2)}, u32[]{:S(2)}) async-start(f32[32,32,256]{2,1,0:T(8,128)} %broadcast_multiply_fusion), calls=%async_computation.2 | async-start | bytes 2097152 | tf_op jit(solution)/shard_map/all_to_all | solution.py:145
  134.9 37.2 %all-reduce.3.cloned.1.call-start = ((), (), s32[]{:S(2)}) async-start(), calls=%async_computation.3 | async-start | bytes 524288 | tf_op jit(solution)/shard_map/psum | solution.py:14
  136.9 109.6 %all-reduce.5.cloned.1.call-start = ((), (), s32[]{:S(2)}) async-start(), calls=%async_computation.4 | async-start | bytes 524288 | tf_op jit(solution)/shard_map/psum | solution.py:15
Sparse Core Ops, SparseCore 0:
  138.7 33.4 all-reduce.2
  175.8 70.5 all-reduce.4
